TPU v7x, 512 devices: a whole 4x4x16 slice. The times are simulated.
512 devices in a mesh: dp: 16 (over y_lo, x, core), mp: 32 (over z, y_hi).
Axes of the slice: x: 4, y: 4 (y_hi: 2, y_lo: 2; y = y_hi * 2 + y_lo), z: 16, core: 2. Of those that a mesh axis runs over, the one named last changes fastest.
Arguments:
- hidden_states: bfloat16 [8192, 2560], P(('dp', 'mp')), may hold values from -60 to 60
- norm_gain: float32 [2560], replicated, may hold values from 0.5 to 1.5
- head_weight: bfloat16 [2560, 65536], P(None, ('dp', 'mp')), may hold values from -64 to 64
- target_ids: int32 [8192], P(('dp', 'mp')), may hold values from 0 to 65535
- response_mask: int32 [8192], P(('dp', 'mp')), may hold values from 0 to 1, as said below
Outputs:
- token_logprob: float32 [8192], P(('dp', 'mp'))
- token_entropy: float32 [8192], P(('dp', 'mp'))
Inputs may be any that keep to these rules, and one draw needn't show every extreme that they name: `response_mask`: each aligned run of 256 positions is one rollout: a prompt of 0s, then one span of 1s, then padding 0s.
All inputs are finite; a program needn't handle non-finite values.
Results may differ from a plain program's by a relative error of at most 0.0048.
Values may be sent and summed in bfloat16 or wider, within the bound.
No kernel may reach another device: no remote copies, remote signals or barrier semaphores. Data moves between devices by JAX's collectives and lax.ppermute only.
A program may use at most 64 MiB of HBM per device.

v0:
```python
import jax
import jax.numpy as jnp
from jax import lax
from jax.sharding import PartitionSpec as P

id_base = 256


def local(hidden_states, norm_gain, head_weight, target_ids, response_mask):
    states = hidden_states.astype(jnp.float32)
    mean_square = jnp.mean(states * states, axis=1, keepdims=True)
    normed = (states * lax.rsqrt(mean_square + 1e-06) * norm_gain[None, :]).astype(jnp.bfloat16)
    width = normed.shape[1]
    mp_count = lax.axis_size("mp")
    mp_index = lax.axis_index("mp")
    shard_cols = head_weight.shape[1]
    send_count = normed.shape[0]
    id_high = (target_ids // id_base).astype(jnp.bfloat16)
    id_low = (target_ids % id_base).astype(jnp.bfloat16)
    packed = jnp.concatenate([normed, id_high[:, None], id_low[:, None]], axis=1)
    group = lax.all_gather(packed, "mp", axis=0, tiled=True)
    group_states = group[:, :width]
    group_targets = group[:, width].astype(jnp.int32) * id_base + group[:, width + 1].astype(
        jnp.int32
    )
    column_piece = lax.all_gather(head_weight, "dp", axis=1, tiled=True)
    positions = jnp.arange(column_piece.shape[1], dtype=jnp.int32)
    owners = positions // shard_cols
    column_ids = (owners * mp_count + mp_index) * shard_cols + positions % shard_cols
    logits = jnp.dot(group_states, column_piece, preferred_element_type=jnp.float32)
    top = jnp.max(logits, axis=1)
    shifted = jnp.exp(logits - top[:, None])
    total = jnp.sum(shifted, axis=1)
    moment = jnp.sum(shifted * logits, axis=1)
    hit = group_targets[:, None] == column_ids[None, :]
    chosen = jnp.sum(jnp.where(hit, logits, 0.0), axis=1)
    part_lse = top + jnp.log(total)
    part_expected = moment / total
    stats = jnp.stack([part_lse, part_expected, chosen], axis=0)
    stats = stats.reshape(3, mp_count, send_count)
    got = lax.all_to_all(stats, "mp", split_axis=1, concat_axis=1, tiled=True)
    lse_parts, expected_parts, chosen_parts = (got[0], got[1], got[2])
    top_lse = jnp.max(lse_parts, axis=0)
    log_total = top_lse + jnp.log(jnp.sum(jnp.exp(lse_parts - top_lse[None, :]), axis=0))
    weights = jnp.exp(lse_parts - log_total[None, :])
    expected = jnp.sum(weights * expected_parts, axis=0)
    chosen_logit = jnp.sum(chosen_parts, axis=0)
    scored = response_mask.astype(jnp.float32)
    return ((chosen_logit - log_total) * scored, (log_total - expected) * scored)


def solution(mesh):
    return jax.shard_map(
        local,
        mesh=mesh,
        in_specs=(
            P(("dp", "mp"), None),
            P(),
            P(None, ("dp", "mp")),
            P(("dp", "mp")),
            P(("dp", "mp")),
        ),
        out_specs=(P(("dp", "mp")), P(("dp", "mp"))),
        check_vma=False,
    )
```

profile of v0, /device:TPU:2, one launch (start us, length us, event | category | flops | bytes accessed | tf_op | source)
XLA Modules:
  0.0 291.5 jit_solution(14386886251495838894)
XLA Ops:
  7.2 0.0 all-gather.3.cloned.1.call-start
  7.2 0.7 fusion.18
  7.9 0.1 copy.11
  8.0 0.1 copy.12
  8.1 1.0 fusion.3
  9.1 1.0 fusion.5
  10.1 0.7 concatenate.4
  10.8 0.0 all-gather.3.cloned.1.call-update
  10.8 0.0 all-gather.5.cloned.1.call-start
  10.9 0.7 all-gather.5.cloned.1.call-update
  11.6 158.5 %all-gather.3.cloned.1.call-done = bf16[512,2562]{1,0:T(8,128)(2,1)} async-done(((bf16[16,2562]{1,0:T(8,128)(2,1)}), bf16[512,2562]{1,0:T(8,128)(2,1)}) %all-gather.3.cloned.1.call-update) | async-done | bytes 2623504 | tf_op jit(solution)/shard_map/all_gather | solution.py:21
  170.1 1.2 add_reduce_fusion
  171.3 71.3 %all-gather.5.cloned.1.call-done = bf16[2560,2048]{1,0:T(8,128)(2,1)} async-done(((bf16[2560,128]{1,0:T(8,128)(2,1)}), bf16[2560,2048]{1,0:T(8,128)(2,1)}) %all-gather.5.cloned.1.call-update) | async-done | bytes 10485776 | tf_op jit(solution)/shard_map/all_gather | solution.py:26
  242.6 9.2 %fusion.20 = (f32[512]{0:T(512)S(1)}, f32[512,2048]{1,0:T(8,128)S(1)}) fusion(bf16[2560,2048]{1,0:T(8,128)(2,1)} %all-gather.5.cloned.1.call-done, bf16[512,2562]{1,0:T(8,128)(2,1)} %all-gather.3.cloned.1.call-done), kind=kOutput, calls=%fused_computation.45 | convolution fusion | flops 5369757184 | bytes 17303552 | tf_op jit(solution)/shard_map/dot_general | solution.py:30
  251.8 0.0 copy-start
  251.8 1.8 fusion
  253.7 0.1 add.75
  253.8 0.1 div.43
  253.9 0.1 stack.8
  254.0 29.5 %all_to_all.5 = f32[3,32,16]{2,0,1:T(4,128)S(1)} all-to-all(f32[3,32,16]{2,0,1:T(4,128)S(1)} %copy.13), channel_id=1, replica_groups=mesh['dp'=16,'mp'=32] {'mp'}, dimensions={1} | all-to-all | bytes 12288 | tf_op jit(solution)/shard_map/all_to_all | solution.py:41
  283.5 0.1 fusion.19
  283.6 0.0 copy-done
  283.6 0.5 convert_multiply_fusion.2
  284.1 0.5 subtract_multiply_fusion
  (8 shorter events, 0.2 us)
Async XLA Ops:
  7.2 163.0 %all-gather.3.cloned.1.call-start = ((), (), s32[]{:S(2)}) async-start(), calls=%async_computation.1 | async-start | bytes 2838528 | tf_op jit(solution)/shard_map/all_gather | solution.py:21
  10.8 231.8 %all-gather.5.cloned.1.call-start = ((), (), s32[]{:S(2)}) async-start(), calls=%async_computation.2 | async-start | bytes 11141120 | tf_op jit(solution)/shard_map/all_gather | solution.py:26
  251.8 31.7 %copy-start = (s32[16]{0:T(128)S(1)}, s32[16]{0:T(128)}, u32[]{:S(2)}) copy-start(s32[16]{0:T(128)} %param.9) | copy-start | bytes 196
Sparse Core Ops, SparseCore 0:
  11.1 158.9 all-gather.2
  172.2 70.3 all-gather.4
where the time goes:
time: 292 us; the launch traced here: 291 us
  waiting for transfers between devices  230 us (79%)
  blocking collectives  29.5 us (10%)
  between operations  14.1 us (5%)
  matrix products  9.23 us (3%)
  other arithmetic  6.95 us (2%)
    all_gather x1, waiting for transfers between devices, local(): group = lax.all_gather(packed, 'mp', axis=0, tiled=True)  159 us
    all_gather x1, waiting for transfers between devices, local(): column_piece = lax.all_gather(head_weight, 'dp', axis=1, tiled=True)  71.3 us
    all_to_all x1, blocking collectives, local(): got = lax.all_to_all(stats, 'mp', split_axis=1, concat_axis=1, tiled=True)  29.5 us
    dot_general x1, matrix products, local(): jnp.dot(group_states, column_piece, preferred_element_type=jnp.float32)  9.23 us
  transfers between devices with their start and end apart: 2, of which 2 were waited for; matrix products, arithmetic and copies ran while one was open for 0% of the time, Pallas kernels for 0%

commit v1 on v0

--- a/solution.py
+++ b/solution.py
@@ -38,7 +38,15 @@
     part_expected = moment / total
     stats = jnp.stack([part_lse, part_expected, chosen], axis=0)
     stats = stats.reshape(3, mp_count, send_count)
-    got = lax.all_to_all(stats, "mp", split_axis=1, concat_axis=1, tiled=True)
+    got = jnp.concatenate(
+        jax.lax.all_to_all(
+            jnp.stack(jnp.split(stats, jax.lax.axis_size("mp"), 1)),
+            axis_name="mp",
+            split_axis=0,
+            concat_axis=0,
+        ),
+        1,
+    )
     lse_parts, expected_parts, chosen_parts = (got[0], got[1], got[2])
     top_lse = jnp.max(lse_parts, axis=0)
     log_total = top_lse + jnp.log(jnp.sum(jnp.exp(lse_parts - top_lse[None, :]), axis=0))

time: 292 us -> 292 us (level)
  the two profiles are of different devices: /device:TPU:2 before, /device:TPU:1 now
where the time goes in v1:
time: 292 us; the launch traced here: 291 us
  waiting for transfers between devices  233 us (80%)
  blocking collectives  27.1 us (9%)
  between operations  14.1 us (5%)
  matrix products  9.23 us (3%)
  other arithmetic  6.94 us (2%)
    all_gather x1, waiting for transfers between devices, local(): group = lax.all_gather(packed, 'mp', axis=0, tiled=True)  149 us
    all_gather x1, waiting for transfers between devices, local(): column_piece = lax.all_gather(head_weight, 'dp', axis=1, tiled=True)  82.5 us
    all_to_all x1, blocking collectives, local(): jax.lax.all_to_all(jnp.stack(jnp.split(stats, jax.lax.axis_size('mp'), 1)...  27.1 us
    dot_general x1, matrix products, local(): jnp.dot(group_states, column_piece, preferred_element_type=jnp.float32)  9.23 us
  transfers between devices with their start and end apart: 2, of which 2 were waited for; matrix products, arithmetic and copies ran while one was open for 0% of the time, Pallas kernels for 0%

profile of v1, /device:TPU:1, one launch (start us, length us, event | category | flops | bytes accessed | tf_op | source)
XLA Modules:
  0.0 291.4 jit_solution(6846925871470071664)
XLA Ops:
  7.2 0.0 all-gather.3.cloned.1.call-start
  7.2 0.7 fusion.18
  7.9 0.1 copy.17
  8.0 0.1 copy.18
  8.1 1.0 fusion.3
  9.1 1.0 fusion.5
  10.1 0.7 concatenate.4
  10.8 0.0 all-gather.3.cloned.1.call-update
  10.8 0.0 all-gather.5.cloned.1.call-start
  10.9 0.7 all-gather.5.cloned.1.call-update
  11.6 149.3 %all-gather.3.cloned.1.call-done = bf16[512,2562]{1,0:T(8,128)(2,1)} async-done(((bf16[16,2562]{1,0:T(8,128)(2,1)}), bf16[512,2562]{1,0:T(8,128)(2,1)}) %all-gather.3.cloned.1.call-update) | async-done | bytes 2623504 | tf_op jit(solution)/shard_map/all_gather | solution.py:21
  160.9 1.2 add_reduce_fusion
  162.1 82.5 %all-gather.5.cloned.1.call-done = bf16[2560,2048]{1,0:T(8,128)(2,1)} async-done(((bf16[2560,128]{1,0:T(8,128)(2,1)}), bf16[2560,2048]{1,0:T(8,128)(2,1)}) %all-gather.5.cloned.1.call-update) | async-done | bytes 10485776 | tf_op jit(solution)/shard_map/all_gather | solution.py:26
  244.6 9.2 %fusion.21 = (f32[512]{0:T(512)S(1)}, f32[512,2048]{1,0:T(8,128)S(1)}) fusion(bf16[2560,2048]{1,0:T(8,128)(2,1)} %all-gather.5.cloned.1.call-done, bf16[512,2562]{1,0:T(8,128)(2,1)} %all-gather.3.cloned.1.call-done), kind=kOutput, calls=%fused_computation.80 | convolution fusion | flops 5369757184 | bytes 17303552 | tf_op jit(solution)/shard_map/dot_general | solution.py:30
  253.9 0.0 copy-start
  253.9 1.9 multiply_reduce_fusion
  255.8 0.1 add.75
  255.8 0.1 div.43
  255.9 0.1 stack.107
  256.1 0.1 stack.141
  256.2 0.1 copy.19
  256.3 27.1 %all_to_all.5 = f32[32,3,1,16]{3,2,1,0:T(1,128)S(1)} all-to-all(f32[32,3,1,16]{3,2,1,0:T(1,128)S(1)} %copy.19), channel_id=1, replica_groups=mesh['dp'=16,'mp'=32] {'mp'}, dimensions={0} | all-to-all | bytes 12288 | tf_op jit(solution)/shard_map/all_to_all | solution.py:42
  283.3 0.1 fusion.19
  283.5 0.0 copy-done
  283.5 0.5 convert_multiply_fusion.2
  284.0 0.5 subtract_multiply_fusion
  (11 shorter events, 0.2 us)
Async XLA Ops:
  7.2 153.8 %all-gather.3.cloned.1.call-start = ((), (), s32[]{:S(2)}) async-start(), calls=%async_computation.1 | async-start | bytes 2838528 | tf_op jit(solution)/shard_map/all_gather | solution.py:21
  10.8 233.8 %all-gather.5.cloned.1.call-start = ((), (), s32[]{:S(2)}) async-start(), calls=%async_computation.2 | async-start | bytes 11141120 | tf_op jit(solution)/shard_map/all_gather | solution.py:26
  253.9 29.6 %copy-start = (s32[16]{0:T(128)S(1)}, s32[16]{0:T(128)}, u32[]{:S(2)}) copy-start(s32[16]{0:T(128)} %param.9) | copy-start | bytes 196
Sparse Core Ops, SparseCore 0:
  11.1 149.7 all-gather.2
  163.0 81.5 all-gather.4

commit v2 on v0

--- a/solution.py
+++ b/solution.py
@@ -2,6 +2,7 @@
 import jax.numpy as jnp
 from jax import lax
 from jax.sharding import PartitionSpec as P
+from jax.lax import all_to_all, psum
 
 id_base = 256
 
@@ -23,7 +24,10 @@
     group_targets = group[:, width].astype(jnp.int32) * id_base + group[:, width + 1].astype(
         jnp.int32
     )
-    column_piece = lax.all_gather(head_weight, "dp", axis=1, tiled=True)
+    x_next = tuple((head_weight for _ in range(psum(1, "dp"))))
+    plain = jnp.stack(x_next, axis=0)
+    f_next = all_to_all(plain, "dp", 0, 0)
+    column_piece = jnp.concatenate(f_next, axis=1)
     positions = jnp.arange(column_piece.shape[1], dtype=jnp.int32)
     owners = positions // shard_cols
     column_ids = (owners * mp_count + mp_index) * shard_cols + positions % shard_cols

time: 292 us -> 261 us (0.89)
  the two profiles are of different devices: /device:TPU:2 before, /device:TPU:4 now
where the time goes in v2:
time: 261 us; the launch traced here: 260 us
  waiting for transfers between devices  192 us (74%)
  blocking collectives  22.2 us (9%)
  between operations  14.1 us (5%)
  starting transfers between devices  10.6 us (4%)
  matrix products  9.3 us (4%)
  local copies, waits for them, and re-layouts  7.37 us (3%)
  other arithmetic  4.49 us (2%)
    all_gather x1, waiting for transfers between devices, local(): group = lax.all_gather(packed, 'mp', axis=0, tiled=True)  192 us
    all_to_all x1, blocking collectives, local(): got = lax.all_to_all(stats, 'mp', split_axis=1, concat_axis=1, tiled=True)  22.2 us
    all_to_all x1, starting transfers between devices, local(): f_next = all_to_all(plain, 'dp', 0, 0)  10.6 us
    dot_general x1, matrix products, local(): jnp.dot(group_states, column_piece, preferred_element_type=jnp.float32)  9.3 us
  transfers between devices with their start and end apart: 2, of which 1 were waited for; matrix products, arithmetic and copies ran while one was open for 1% of the time, Pallas kernels for 0%

profile of v2, /device:TPU:4, one launch (start us, length us, event | category | flops | bytes accessed | tf_op | source)
XLA Modules:
  0.0 260.4 jit_solution(5523966106459552576)
XLA Ops:
  7.2 1.3 copy.14
  8.5 4.8 %stack.6 = bf16[16,2560,128]{1,2,0:T(8,128)(2,1)} broadcast(bf16[2560,128]{0,1:T(8,128)(2,1)S(1)} %copy.14), dimensions={1,2} | broadcast | bytes 11141120 | tf_op jit(solution)/shard_map/stack | solution.py:28
  13.3 0.0 copy-start.3
  13.3 0.0 copy-start
  13.3 0.0 copy-start.1
  13.4 10.6 %all-to-all-start = ((bf16[16,2560,128]{1,2,0:T(8,128)(2,1)}), bf16[16,2560,128]{1,2,0:T(8,128)(2,1)}, u32[]{:S(2)}, u32[]{:S(2)}) async-start(bf16[16,2560,128]{1,2,0:T(8,128)(2,1)} %stack.6), calls=%async_computation | async-start | bytes 20971520 | tf_op jit(solution)/shard_map/all_to_all | solution.py:29
  23.9 0.0 all-gather.2.cloned.1.call-start
  24.0 0.0 copy-done.3
  24.0 0.1 copy.12
  24.1 0.1 copy.13
  24.2 0.0 copy-done
  24.2 0.1 fusion.3
  24.3 0.0 copy-done.1
  24.3 0.1 fusion.5
  24.4 0.7 concatenate.4
  25.1 0.0 all-gather.2.cloned.1.call-update
  25.2 192.3 %all-gather.2.cloned.1.call-done = bf16[512,2562]{1,0:T(8,128)(2,1)} async-done(((bf16[16,2562]{1,0:T(8,128)(2,1)}), bf16[512,2562]{1,0:T(8,128)(2,1)}) %all-gather.2.cloned.1.call-update) | async-done | bytes 2623504 | tf_op jit(solution)/shard_map/all_gather | solution.py:22
  217.5 1.2 add_reduce_fusion
  218.7 0.0 all-to-all-done
  218.7 9.3 %fusion.20 = (f32[512]{0:T(512)S(1)}, f32[512,2048]{1,0:T(8,128)S(1)}) fusion(bf16[2560,2048]{0,1:T(8,128)(2,1)} %bitcast.3, bf16[512,2562]{1,0:T(8,128)(2,1)} %all-gather.2.cloned.1.call-done), kind=kOutput, calls=%fused_computation.45 | convolution fusion | flops 5369757184 | bytes 17303552 | tf_op jit(solution)/shard_map/dot_general | solution.py:34
  228.0 0.0 copy-start.2
  228.0 1.8 fusion
  229.8 0.1 stack.7
  229.9 0.1 div.43
  230.0 0.1 add.75
  230.1 22.2 %all_to_all.10 = f32[3,32,16]{2,0,1:T(4,128)S(1)} all-to-all(f32[3,32,16]{2,0,1:T(4,128)S(1)} %copy.15), channel_id=1, replica_groups=mesh['dp'=16,'mp'=32] {'mp'}, dimensions={1} | all-to-all | bytes 12288 | tf_op jit(solution)/shard_map/all_to_all | solution.py:45
  252.3 0.1 fusion.19
  252.4 0.0 copy-done.2
  252.4 0.5 convert_multiply_fusion.2
  253.0 0.5 subtract_multiply_fusion
  (9 shorter events, 0.2 us)
Async XLA Ops:
  13.3 10.6 %copy-start.3 = (s32[16]{0:T(128)S(1)}, s32[16]{0:T(128)}, u32[]{:S(2)}) copy-start(s32[16]{0:T(128)} %param.8) | copy-start | bytes 196
  13.3 10.8 %copy-start = (bf16[16,2560]{1,0:T(8,128)(2,1)S(1)}, bf16[16,2560]{1,0:T(8,128)(2,1)}, u32[]{:S(2)}) copy-start(bf16[16,2560]{1,0:T(8,128)(2,1)} %param.5) | copy-start | bytes 245764
  13.3 11.0 %copy-start.1 = (f32[2560]{0:T(1024)S(1)}, f32[2560]{0:T(1024)}, u32[]{:S(2)}) copy-start(f32[2560]{0:T(1024)} %param.6) | copy-start | bytes 30724
  13.4 205.3 %all-to-all-start = ((bf16[16,2560,128]{1,2,0:T(8,128)(2,1)}), bf16[16,2560,128]{1,2,0:T(8,128)(2,1)}, u32[]{:S(2)}, u32[]{:S(2)}) async-start(bf16[16,2560,128]{1,2,0:T(8,128)(2,1)} %stack.6), calls=%async_computation | async-start | bytes 20971520 | tf_op jit(solution)/shard_map/all_to_all | solution.py:29
  23.9 193.5 %all-gather.2.cloned.1.call-start = ((), (), s32[]{:S(2)}) async-start(), calls=%async_computation.2 | async-start | bytes 2838528 | tf_op jit(solution)/shard_map/all_gather | solution.py:22
  228.0 24.5 %copy-start.2 = (s32[16]{0:T(128)S(1)}, s32[16]{0:T(128)}, u32[]{:S(2)}) copy-start(s32[16]{0:T(128)} %param.9) | copy-start | bytes 196
Sparse Core Ops, SparseCore 0:
  27.9 189.5 all-gather.1
